TPU v7x, 256 devices: a whole 4x4x8 slice. The times are simulated.
256 devices in a mesh: span: 8 (over y, x_hi), tm: 32 (over x_lo, z, core).
Axes of the slice: x: 4 (x_hi: 2, x_lo: 2; x = x_hi * 2 + x_lo), y: 4, z: 8, core: 2. Of those that a mesh axis runs over, the one named last changes fastest.
Arguments:
- launched: float32 [8, 2, 110, 8192], P(None, None, None, 'tm'), may hold values from -1.5 to 1.5
- coupling: float32 [8, 2, 2, 2, 110, 110], P('span'), may hold values from -2 to 2
- impulse: float32 [8, 2, 2, 2, 129], P('span'), may hold values from -1.5 to 1.5
- amplifier: float32 [8, 2, 110], P('span'), may hold values from 0.9 to 1.11
- nonlinear: float32 [8, 2, 2], P('span'), may hold values from 0.002 to 0.008
Outputs:
- monitored: float32 [8, 8, 2, 110, 8192], P('span', None, None, None, 'tm')
All inputs are finite; a program needn't handle non-finite values.
Results may differ from a plain program's by a relative error of at most 0.0004.
Values sent between devices are 32-bit elements; how exact they have to be, the bound alone decides.
No kernel may reach another device: no remote copies, remote signals or barrier semaphores. Data moves between devices by JAX's collectives and lax.ppermute only.
A program may use at most 64 MiB of HBM per device.

v0:
```python
import jax
import jax.numpy as jnp
from jax import lax
from jax.sharding import PartitionSpec as P


def band(values, width):
    padded = jnp.concatenate([values, jnp.zeros((width,), jnp.float32)])
    tiled = jnp.tile(padded, width)[: width * 2 * width]
    return tiled.reshape(width, 2 * width).T


def prepare(coupling_group, impulse_group):
    half_taps = (impulse_group.shape[-1] - 1) // 2
    width = 2 * half_taps

    def toeplitz(pair):
        real_band = band(pair[0], width)
        imag_band = band(pair[1], width)
        upper = jnp.concatenate([real_band, imag_band], axis=1)
        lower = jnp.concatenate([-imag_band, real_band], axis=1)
        return jnp.concatenate([upper, lower], axis=0)

    filters = jax.vmap(jax.vmap(toeplitz))(impulse_group)
    real_part = coupling_group[:, :, 0]
    imag_part = coupling_group[:, :, 1]
    upper = jnp.concatenate([real_part, -imag_part], axis=-1)
    lower = jnp.concatenate([imag_part, real_part], axis=-1)
    return (filters, jnp.concatenate([upper, lower], axis=-2))


def disperse(extended, matrix, half_taps):
    width = 2 * half_taps
    frames, _, channels, extent = extended.shape
    block_count = extent // width - 1
    blocks = extended.reshape(frames, 2, channels, block_count + 1, width)
    windows = jnp.concatenate([blocks[..., :-1, :], blocks[..., 1:, :]], axis=-1)
    stacked = jnp.concatenate([windows[:, 0], windows[:, 1]], axis=-1)
    product = jnp.einsum("fcbu,uv->fcbv", stacked, matrix, precision=lax.Precision.HIGHEST)
    real_part = product[..., :width].reshape(frames, channels, block_count * width)
    imag_part = product[..., width:].reshape(frames, channels, block_count * width)
    return jnp.stack([real_part, imag_part], axis=1)


def couple(signal, mixer, coefficient):
    frames, _, channels, extent = signal.shape
    flat = signal.reshape(frames, 2 * channels, extent)
    mixed = jnp.einsum("de,fel->fdl", mixer, flat, precision=lax.Precision.HIGHEST).reshape(
        frames, 2, channels, extent
    )
    power = jnp.sum(mixed * mixed, axis=(1, 2))
    phase = coefficient * power[:, None, :]
    cosine = jnp.cos(phase)
    sine = jnp.sin(phase)
    real_part = mixed[:, 0]
    imag_part = mixed[:, 1]
    return jnp.stack(
        [real_part * cosine - imag_part * sine, real_part * sine + imag_part * cosine], axis=1
    )


def neighbours(block, halo):
    count = lax.axis_size("tm")
    forward = [(i, i + 1) for i in range(count - 1)]
    backward = [(i + 1, i) for i in range(count - 1)]
    extent = block.shape[-1]
    low = lax.ppermute(lax.slice_in_dim(block, extent - halo, None, axis=3), "tm", forward)
    high = lax.ppermute(lax.slice_in_dim(block, 0, halo, axis=3), "tm", backward)
    return jnp.concatenate([low, block, high], axis=3)


def group_pass(signal, filters, mixers, amplifier_group, nonlinear_group, origin, length):
    span_count, step_count = nonlinear_group.shape
    half_taps = filters.shape[-1] // 4
    halo = span_count * step_count * half_taps
    extent = signal.shape[-1]
    signal = neighbours(signal, halo)
    offset = -halo
    for span_index in range(span_count):
        for step_index in range(step_count):
            signal = disperse(signal, filters[span_index, step_index], half_taps)
            offset = offset + half_taps
            where = origin + offset + jnp.arange(signal.shape[-1], dtype=jnp.int32)
            inside = ((where >= 0) & (where < length)).astype(jnp.float32)
            signal = signal * inside
            signal = couple(
                signal, mixers[span_index, step_index], nonlinear_group[span_index, step_index]
            )
        signal = signal * amplifier_group[span_index][None, None, :, None]
    assert signal.shape[-1] == extent
    return signal


def shards(launched, coupling, impulse, amplifier, nonlinear):
    sections = lax.axis_size("span")
    section_index = lax.axis_index("span")
    frames_count, _, _, extent = launched.shape
    per_section = frames_count // sections
    length = extent * lax.axis_size("tm")
    origin = lax.axis_index("tm") * extent
    coupling_all = lax.all_gather(coupling, "span", axis=0, tiled=True)
    impulse_all = lax.all_gather(impulse, "span", axis=0, tiled=True)
    amplifier_all = lax.all_gather(amplifier, "span", axis=0, tiled=True)
    nonlinear_all = lax.all_gather(nonlinear, "span", axis=0, tiled=True)
    signal = lax.dynamic_slice_in_dim(launched, section_index * per_section, per_section, 0)

    def advance(signal, params):
        coupling_group, impulse_group, amplifier_group, nonlinear_group = params
        filters, mixers = prepare(coupling_group, impulse_group)
        signal = group_pass(
            signal, filters, mixers, amplifier_group, nonlinear_group, origin, length
        )
        return (signal, signal)

    _, stacked = lax.scan(
        advance, signal, (coupling_all, impulse_all, amplifier_all, nonlinear_all)
    )
    return lax.all_to_all(stacked, "span", 0, 1, tiled=True)


def solution(mesh):
    placed = (
        P(None, None, None, "tm"),
        P("span", None, None, None, None, None),
        P("span", None, None, None, None),
        P("span", None, None),
        P("span", None, None),
    )
    return jax.shard_map(
        shards,
        mesh=mesh,
        in_specs=placed,
        out_specs=P("span", None, None, None, "tm"),
        check_vma=False,
    )
```

profile of v0, /device:TPU:2, one launch (start us, length us, event | category | flops | bytes accessed | tf_op | source)
XLA Modules:
  0.0 689.6 jit_solution(1994653478486105164)
XLA Ops:
  8.7 22.9 %all_gather.14 = f32[8,2,2]{2,1,0:T(2,128)S(1)} all-gather(f32[1,2,2]{2,1,0:T(2,128)} %param.11), channel_id=1, replica_groups=mesh['span'=8,'tm'=32] {'span'}, dimensions={0}, use_global_device_ids=true | all-gather | bytes 144 | tf_op jit(solution)/shard_map/all_gather | solution.py:104
  31.7 18.4 %all_gather.15 = f32[8,2,110]{2,1,0:T(2,128)S(1)} all-gather(f32[1,2,110]{2,1,0:T(2,128)} %param.10), channel_id=1, replica_groups=mesh['span'=8,'tm'=32] {'span'}, dimensions={0}, use_global_device_ids=true | all-gather | bytes 7920 | tf_op jit(solution)/shard_map/all_gather | solution.py:103
  50.1 37.0 %all_gather.12 = f32[8,2,2,2,129]{4,3,2,1,0:T(2,128)} all-gather(f32[1,2,2,2,129]{4,3,2,1,0:T(2,128)} %param.9), channel_id=1, replica_groups=mesh['span'=8,'tm'=32] {'span'}, dimensions={0}, use_global_device_ids=true | all-gather | bytes 37152 | tf_op jit(solution)/shard_map/all_gather | solution.py:102
  87.1 568.2 %while.13 = (s32[]{:T(128)}, f32[1,2,110,256]{3,2,1,0:T(8,128)}, f32[8,1,2,110,256]{4,2,3,1,0:T(2,128)}, f32[8,2,2,2,129]{4,3,2,1,0:T(2,128)}, s32[]{:T(128)}, /...) while((s32[]{:T(128)}, f32[1,2,110,256]{3,2,1,0:T(8,128)}, ...), condition=%wide.region_5.6_spmd, body=%wide.region_0.5_spmd.sunk | while | flops 3470978304 | bytes 83243504 | solution.py:115
  89.0 2.4 collective-permute-start.1
  106.0 2.7 maximum_maximum_fusion.4
  138.9 2.4 multiply_reduce_fusion.9
  154.8 8.4 %collective-permute-start = (f32[1,2,110,256]{3,2,1,0:T(8,128)}, f32[1,2,110,256]{3,2,1,0:T(8,128)}, u32[]{:S(2)}, u32[]{:S(2)}) collective-permute-start(f32[1,2,110,256]{3,2,1,0:T(8,128)} %get-tuple-element.367), channel_id=1, source_target_pairs={{1,0},{2,1},{3,2},{4,3},{5,4},{6,5},{7,6},{8,7},{9,8},{10,9},{11,1... | collective-permute-start | bytes 675848 | tf_op jit(solution)/shard_map/while/body/eval_jaxpr/ppermute | solution.py:68
  179.8 2.7 maximum_maximum_fusion.4
  212.6 2.4 multiply_reduce_fusion.9
  228.6 5.7 collective-permute-start
  245.8 2.3 reshape.881
  250.9 2.7 maximum_maximum_fusion.4
  283.7 2.4 multiply_reduce_fusion.9
  299.7 5.7 collective-permute-start
  322.0 2.7 maximum_maximum_fusion.4
  354.8 2.4 multiply_reduce_fusion.9
  370.8 5.7 collective-permute-start
  388.0 2.3 reshape.881
  393.1 2.7 maximum_maximum_fusion.4
  426.0 2.4 multiply_reduce_fusion.9
  441.9 5.7 collective-permute-start
  459.1 2.3 reshape.881
  464.2 2.7 maximum_maximum_fusion.4
  497.1 2.4 multiply_reduce_fusion.9
  513.0 5.7 collective-permute-start
  535.3 2.7 maximum_maximum_fusion.4
  568.2 2.4 multiply_reduce_fusion.9
  584.1 5.7 collective-permute-start
  606.4 2.7 maximum_maximum_fusion.4
  639.3 2.4 multiply_reduce_fusion.9
  655.2 26.3 %all_to_all.12 = f32[8,1,2,110,256]{4,2,3,1,0:T(2,128)S(1)} all-to-all(f32[8,1,2,110,256]{4,2,3,1,0:T(2,128)} %get-tuple-element.90), channel_id=1, replica_groups=mesh['span'=8,'tm'=32] {'span'}, dimensions={0} | all-to-all | bytes 3604480 | tf_op jit(solution)/shard_map/all_to_all | solution.py:118
  (894 shorter events, 475.0 us)
Async XLA Ops:
  6.5 80.5 %all-gather.2.cloned.1.call-start = ((), (), s32[]{:S(2)}) async-start(), calls=%async_computation.1 | async-start | bytes 4055040 | tf_op jit(solution)/shard_map/all_gather | solution.py:101
  87.1 22.0 %collective-permute-start = (f32[1,2,110,256]{3,2,1,0:T(8,128)}, f32[1,2,110,256]{3,2,1,0:T(8,128)}, u32[]{:S(2)}, u32[]{:S(2)}) collective-permute-start(f32[1,2,110,256]{3,2,1,0:T(8,128)} %get-tuple-element.367), channel_id=1, source_target_pairs={{1,0},{2,1},{3,2},{4,3},{5,4},{6,5},{7,6},{8,7},{9,8},{10,9},{11,1... | collective-permute-start | bytes 675848 | tf_op jit(solution)/shard_map/while/body/eval_jaxpr/ppermute | solution.py:68
  89.0 20.1 %collective-permute-start.1 = (f32[1,2,110,256]{3,2,1,0:T(8,128)}, f32[1,2,110,256]{3,2,1,0:T(8,128)}, u32[]{:S(2)}, u32[]{:S(2)}) collective-permute-start(f32[1,2,110,256]{3,2,1,0:T(8,128)} %get-tuple-element.367), channel_id=1, source_target_pairs={{0,1},{1,2},{2,3},{3,4},{4,5},{5,6},{6,7},{7,8},{8,9},{9,10},{10,1... | collective-permute-start | bytes 675848 | tf_op jit(solution)/shard_map/while/body/eval_jaxpr/ppermute | solution.py:67
  99.1 7.0 %copy-start.1 = (f32[2,2,256,128]{3,2,1,0:T(8,128)S(1)}, f32[2,2,256,128]{3,2,1,0:T(8,128)}, u32[]{:S(2)}) copy-start(f32[2,2,256,128]{3,2,1,0:T(8,128)} %bitcast_negate_fusion.2) | copy-start | bytes 1572868 | tf_op jit(solution)/shard_map/while
  105.4 3.3 copy-start.4
  154.8 27.9 %collective-permute-start = (f32[1,2,110,256]{3,2,1,0:T(8,128)}, f32[1,2,110,256]{3,2,1,0:T(8,128)}, u32[]{:S(2)}, u32[]{:S(2)}) collective-permute-start(f32[1,2,110,256]{3,2,1,0:T(8,128)} %get-tuple-element.367), channel_id=1, source_target_pairs={{1,0},{2,1},{3,2},{4,3},{5,4},{6,5},{7,6},{8,7},{9,8},{10,9},{11,1... | collective-permute-start | bytes 675848 | tf_op jit(solution)/shard_map/while/body/eval_jaxpr/ppermute | solution.py:68
  163.2 19.6 %collective-permute-start.1 = (f32[1,2,110,256]{3,2,1,0:T(8,128)}, f32[1,2,110,256]{3,2,1,0:T(8,128)}, u32[]{:S(2)}, u32[]{:S(2)}) collective-permute-start(f32[1,2,110,256]{3,2,1,0:T(8,128)} %get-tuple-element.367), channel_id=1, source_target_pairs={{0,1},{1,2},{2,3},{3,4},{4,5},{5,6},{6,7},{7,8},{8,9},{9,10},{10,1... | collective-permute-start | bytes 675848 | tf_op jit(solution)/shard_map/while/body/eval_jaxpr/ppermute | solution.py:67
  172.8 7.0 %copy-start.1 = (f32[2,2,256,128]{3,2,1,0:T(8,128)S(1)}, f32[2,2,256,128]{3,2,1,0:T(8,128)}, u32[]{:S(2)}) copy-start(f32[2,2,256,128]{3,2,1,0:T(8,128)} %bitcast_negate_fusion.2) | copy-start | bytes 1572868 | tf_op jit(solution)/shard_map/while
  179.1 3.3 copy-start.4
  228.6 25.3 %collective-permute-start = (f32[1,2,110,256]{3,2,1,0:T(8,128)}, f32[1,2,110,256]{3,2,1,0:T(8,128)}, u32[]{:S(2)}, u32[]{:S(2)}) collective-permute-start(f32[1,2,110,256]{3,2,1,0:T(8,128)} %get-tuple-element.367), channel_id=1, source_target_pairs={{1,0},{2,1},{3,2},{4,3},{5,4},{6,5},{7,6},{8,7},{9,8},{10,9},{11,1... | collective-permute-start | bytes 675848 | tf_op jit(solution)/shard_map/while/body/eval_jaxpr/ppermute | solution.py:68
  234.3 19.6 %collective-permute-start.1 = (f32[1,2,110,256]{3,2,1,0:T(8,128)}, f32[1,2,110,256]{3,2,1,0:T(8,128)}, u32[]{:S(2)}, u32[]{:S(2)}) collective-permute-start(f32[1,2,110,256]{3,2,1,0:T(8,128)} %get-tuple-element.367), channel_id=1, source_target_pairs={{0,1},{1,2},{2,3},{3,4},{4,5},{5,6},{6,7},{7,8},{8,9},{9,10},{10,1... | collective-permute-start | bytes 675848 | tf_op jit(solution)/shard_map/while/body/eval_jaxpr/ppermute | solution.py:67
  243.9 7.0 %copy-start.1 = (f32[2,2,256,128]{3,2,1,0:T(8,128)S(1)}, f32[2,2,256,128]{3,2,1,0:T(8,128)}, u32[]{:S(2)}) copy-start(f32[2,2,256,128]{3,2,1,0:T(8,128)} %bitcast_negate_fusion.2) | copy-start | bytes 1572868 | tf_op jit(solution)/shard_map/while
  250.2 3.3 copy-start.4
  299.7 25.3 %collective-permute-start = (f32[1,2,110,256]{3,2,1,0:T(8,128)}, f32[1,2,110,256]{3,2,1,0:T(8,128)}, u32[]{:S(2)}, u32[]{:S(2)}) collective-permute-start(f32[1,2,110,256]{3,2,1,0:T(8,128)} %get-tuple-element.367), channel_id=1, source_target_pairs={{1,0},{2,1},{3,2},{4,3},{5,4},{6,5},{7,6},{8,7},{9,8},{10,9},{11,1... | collective-permute-start | bytes 675848 | tf_op jit(solution)/shard_map/while/body/eval_jaxpr/ppermute | solution.py:68
  305.4 19.6 %collective-permute-start.1 = (f32[1,2,110,256]{3,2,1,0:T(8,128)}, f32[1,2,110,256]{3,2,1,0:T(8,128)}, u32[]{:S(2)}, u32[]{:S(2)}) collective-permute-start(f32[1,2,110,256]{3,2,1,0:T(8,128)} %get-tuple-element.367), channel_id=1, source_target_pairs={{0,1},{1,2},{2,3},{3,4},{4,5},{5,6},{6,7},{7,8},{8,9},{9,10},{10,1... | collective-permute-start | bytes 675848 | tf_op jit(solution)/shard_map/while/body/eval_jaxpr/ppermute | solution.py:67
  315.0 7.0 %copy-start.1 = (f32[2,2,256,128]{3,2,1,0:T(8,128)S(1)}, f32[2,2,256,128]{3,2,1,0:T(8,128)}, u32[]{:S(2)}) copy-start(f32[2,2,256,128]{3,2,1,0:T(8,128)} %bitcast_negate_fusion.2) | copy-start | bytes 1572868 | tf_op jit(solution)/shard_map/while
  321.3 3.3 copy-start.4
  370.8 25.3 %collective-permute-start = (f32[1,2,110,256]{3,2,1,0:T(8,128)}, f32[1,2,110,256]{3,2,1,0:T(8,128)}, u32[]{:S(2)}, u32[]{:S(2)}) collective-permute-start(f32[1,2,110,256]{3,2,1,0:T(8,128)} %get-tuple-element.367), channel_id=1, source_target_pairs={{1,0},{2,1},{3,2},{4,3},{5,4},{6,5},{7,6},{8,7},{9,8},{10,9},{11,1... | collective-permute-start | bytes 675848 | tf_op jit(solution)/shard_map/while/body/eval_jaxpr/ppermute | solution.py:68
  376.5 19.6 %collective-permute-start.1 = (f32[1,2,110,256]{3,2,1,0:T(8,128)}, f32[1,2,110,256]{3,2,1,0:T(8,128)}, u32[]{:S(2)}, u32[]{:S(2)}) collective-permute-start(f32[1,2,110,256]{3,2,1,0:T(8,128)} %get-tuple-element.367), channel_id=1, source_target_pairs={{0,1},{1,2},{2,3},{3,4},{4,5},{5,6},{6,7},{7,8},{8,9},{9,10},{10,1... | collective-permute-start | bytes 675848 | tf_op jit(solution)/shard_map/while/body/eval_jaxpr/ppermute | solution.py:67
  386.1 7.0 %copy-start.1 = (f32[2,2,256,128]{3,2,1,0:T(8,128)S(1)}, f32[2,2,256,128]{3,2,1,0:T(8,128)}, u32[]{:S(2)}) copy-start(f32[2,2,256,128]{3,2,1,0:T(8,128)} %bitcast_negate_fusion.2) | copy-start | bytes 1572868 | tf_op jit(solution)/shard_map/while
  441.9 25.3 %collective-permute-start = (f32[1,2,110,256]{3,2,1,0:T(8,128)}, f32[1,2,110,256]{3,2,1,0:T(8,128)}, u32[]{:S(2)}, u32[]{:S(2)}) collective-permute-start(f32[1,2,110,256]{3,2,1,0:T(8,128)} %get-tuple-element.367), channel_id=1, source_target_pairs={{1,0},{2,1},{3,2},{4,3},{5,4},{6,5},{7,6},{8,7},{9,8},{10,9},{11,1... | collective-permute-start | bytes 675848 | tf_op jit(solution)/shard_map/while/body/eval_jaxpr/ppermute | solution.py:68
  447.6 19.6 %collective-permute-start.1 = (f32[1,2,110,256]{3,2,1,0:T(8,128)}, f32[1,2,110,256]{3,2,1,0:T(8,128)}, u32[]{:S(2)}, u32[]{:S(2)}) collective-permute-start(f32[1,2,110,256]{3,2,1,0:T(8,128)} %get-tuple-element.367), channel_id=1, source_target_pairs={{0,1},{1,2},{2,3},{3,4},{4,5},{5,6},{6,7},{7,8},{8,9},{9,10},{10,1... | collective-permute-start | bytes 675848 | tf_op jit(solution)/shard_map/while/body/eval_jaxpr/ppermute | solution.py:67
  457.2 7.0 %copy-start.1 = (f32[2,2,256,128]{3,2,1,0:T(8,128)S(1)}, f32[2,2,256,128]{3,2,1,0:T(8,128)}, u32[]{:S(2)}) copy-start(f32[2,2,256,128]{3,2,1,0:T(8,128)} %bitcast_negate_fusion.2) | copy-start | bytes 1572868 | tf_op jit(solution)/shard_map/while
  463.5 3.3 copy-start.4
  513.0 25.3 %collective-permute-start = (f32[1,2,110,256]{3,2,1,0:T(8,128)}, f32[1,2,110,256]{3,2,1,0:T(8,128)}, u32[]{:S(2)}, u32[]{:S(2)}) collective-permute-start(f32[1,2,110,256]{3,2,1,0:T(8,128)} %get-tuple-element.367), channel_id=1, source_target_pairs={{1,0},{2,1},{3,2},{4,3},{5,4},{6,5},{7,6},{8,7},{9,8},{10,9},{11,1... | collective-permute-start | bytes 675848 | tf_op jit(solution)/shard_map/while/body/eval_jaxpr/ppermute | solution.py:68
  518.8 19.6 %collective-permute-start.1 = (f32[1,2,110,256]{3,2,1,0:T(8,128)}, f32[1,2,110,256]{3,2,1,0:T(8,128)}, u32[]{:S(2)}, u32[]{:S(2)}) collective-permute-start(f32[1,2,110,256]{3,2,1,0:T(8,128)} %get-tuple-element.367), channel_id=1, source_target_pairs={{0,1},{1,2},{2,3},{3,4},{4,5},{5,6},{6,7},{7,8},{8,9},{9,10},{10,1... | collective-permute-start | bytes 675848 | tf_op jit(solution)/shard_map/while/body/eval_jaxpr/ppermute | solution.py:67
  528.3 7.0 %copy-start.1 = (f32[2,2,256,128]{3,2,1,0:T(8,128)S(1)}, f32[2,2,256,128]{3,2,1,0:T(8,128)}, u32[]{:S(2)}) copy-start(f32[2,2,256,128]{3,2,1,0:T(8,128)} %bitcast_negate_fusion.2) | copy-start | bytes 1572868 | tf_op jit(solution)/shard_map/while
  534.6 3.3 copy-start.4
  584.1 25.3 %collective-permute-start = (f32[1,2,110,256]{3,2,1,0:T(8,128)}, f32[1,2,110,256]{3,2,1,0:T(8,128)}, u32[]{:S(2)}, u32[]{:S(2)}) collective-permute-start(f32[1,2,110,256]{3,2,1,0:T(8,128)} %get-tuple-element.367), channel_id=1, source_target_pairs={{1,0},{2,1},{3,2},{4,3},{5,4},{6,5},{7,6},{8,7},{9,8},{10,9},{11,1... | collective-permute-start | bytes 675848 | tf_op jit(solution)/shard_map/while/body/eval_jaxpr/ppermute | solution.py:68
  589.9 19.6 %collective-permute-start.1 = (f32[1,2,110,256]{3,2,1,0:T(8,128)}, f32[1,2,110,256]{3,2,1,0:T(8,128)}, u32[]{:S(2)}, u32[]{:S(2)}) collective-permute-start(f32[1,2,110,256]{3,2,1,0:T(8,128)} %get-tuple-element.367), channel_id=1, source_target_pairs={{0,1},{1,2},{2,3},{3,4},{4,5},{5,6},{6,7},{7,8},{8,9},{9,10},{10,1... | collective-permute-start | bytes 675848 | tf_op jit(solution)/shard_map/while/body/eval_jaxpr/ppermute | solution.py:67
  599.4 7.0 %copy-start.1 = (f32[2,2,256,128]{3,2,1,0:T(8,128)S(1)}, f32[2,2,256,128]{3,2,1,0:T(8,128)}, u32[]{:S(2)}) copy-start(f32[2,2,256,128]{3,2,1,0:T(8,128)} %bitcast_negate_fusion.2) | copy-start | bytes 1572868 | tf_op jit(solution)/shard_map/while
  605.7 3.3 copy-start.4
  (18 other events, 58.2 us)
Sparse Core Ops, SparseCore 0:
  9.9 74.1 all-gather.1
where the time goes:
time: 698 us; the launch traced here: 690 us
  local copies, waits for them, and re-layouts  275 us (39%)
  other arithmetic  132 us (19%)
  blocking collectives  105 us (15%)
  matrix products  98.7 us (14%)
  starting transfers between devices  60.5 us (9%)
  between operations  13.4 us (2%)
    dot_general x32, matrix products, disperse(): jnp.einsum('fcbu,uv->fcbv', stacked, matrix, precision=lax.Precision.HIGH...  59.1 us
    ppermute x8, starting transfers between devices, neighbours(): lax.ppermute(lax.slice_in_dim(block, 0, halo, axis=3), 'tm', backward)  44.6 us
    reshape x32, local copies, waits for them, and re-layouts, band(): return tiled.reshape(width, 2 * width).T  40 us
    dot_general x32, matrix products, couple(): jnp.einsum('de,fel->fdl', mixer, flat, precision=lax.Precision.HIGHEST)  39.6 us
    all_gather x1, blocking collectives, shards(): impulse_all = lax.all_gather(impulse, 'span', axis=0, tiled=True)  37 us
    while x80, local copies, waits for them, and re-layouts  28.2 us
    all_to_all x1, blocking collectives, shards(): return lax.all_to_all(stacked, 'span', 0, 1, tiled=True)  26.3 us
    mul x32, other arithmetic, group_pass(): signal = signal * inside  26.3 us
  transfers between devices with their start and end apart: 17, of which 0 were waited for; matrix products, arithmetic and copies ran while one was open for 20% of the time, Pallas kernels for 0%

commit v1 on v0

--- a/solution.py
+++ b/solution.py
@@ -99,7 +99,9 @@
     length = extent * lax.axis_size("tm")
     origin = lax.axis_index("tm") * extent
     coupling_all = lax.all_gather(coupling, "span", axis=0, tiled=True)
-    impulse_all = lax.all_gather(impulse, "span", axis=0, tiled=True)
+    impulse_all = jnp.concatenate(
+        lax.all_to_all(jnp.stack([impulse] * lax.axis_size("span")), "span", 0, 0), axis=0
+    )
     amplifier_all = lax.all_gather(amplifier, "span", axis=0, tiled=True)
     nonlinear_all = lax.all_gather(nonlinear, "span", axis=0, tiled=True)
     signal = lax.dynamic_slice_in_dim(launched, section_index * per_section, per_section, 0)

time: 698 us -> 664 us (0.951)
  blocking collectives: 105 us -> 68.5 us
  waiting for transfers between devices: 0.75 us -> 26.2 us
  local copies, waits for them, and re-layouts: 275 us -> 255 us
  other arithmetic: 132 us -> 124 us
    all_gather x1 -> x0, blocking collectives: 37 us -> none  [shards(): impulse_all = lax.all_gather(impulse, 'span', axis=0, tiled=True)]
    all_gather x1, waiting for transfers between devices: 0.01 us -> 25.4 us  [shards(): coupling_all = lax.all_gather(coupling, 'span', axis=0, tiled=True)]
    reshape x32, local copies, waits for them, and re-layouts: 40 us -> 25 us  [band(): return tiled.reshape(width, 2 * width).T]
    concatenate x8, other arithmetic: 21.3 us -> 12 us  [toeplitz(): return jnp.concatenate([upper, lower], axis=0)]
    dynamic_slice x40 -> x24, local copies, waits for them, and re-layouts: 14.3 us -> 8.73 us  [shards(): lax.scan(advance, signal, (coupling_all, impulse_all, amplifier_all, nonl...]
  transfers between devices with their start and end apart: 17 -> 18, of which waited for: 0 -> 1; matrix products, arithmetic and copies ran while one was open for 20% -> 17% of each run, Pallas kernels for 0% -> 0%
where the time goes in v1:
time: 664 us; the launch traced here: 656 us
  local copies, waits for them, and re-layouts  255 us (38%)
  other arithmetic  124 us (19%)
  matrix products  98.7 us (15%)
  blocking collectives  68.5 us (10%)
  starting transfers between devices  66.5 us (10%)
  waiting for transfers between devices  26.2 us (4%)
  between operations  13.4 us (2%)
    dot_general x32, matrix products, disperse(): jnp.einsum('fcbu,uv->fcbv', stacked, matrix, precision=lax.Precision.HIGH...  59.1 us
    ppermute x8, starting transfers between devices, neighbours(): lax.ppermute(lax.slice_in_dim(block, 0, halo, axis=3), 'tm', backward)  45.1 us
    dot_general x32, matrix products, couple(): jnp.einsum('de,fel->fdl', mixer, flat, precision=lax.Precision.HIGHEST)  39.7 us
    while x80, local copies, waits for them, and re-layouts  28.4 us
    mul x32, other arithmetic, group_pass(): signal = signal * inside  26.3 us
    all_to_all x1, blocking collectives, shards(): return lax.all_to_all(stacked, 'span', 0, 1, tiled=True)  26.1 us
    mul x48, local copies, waits for them, and re-layouts, group_pass(): signal = signal * inside  26 us
    all_gather x1, waiting for transfers between devices, shards(): coupling_all = lax.all_gather(coupling, 'span', axis=0, tiled=True)  25.4 us
  transfers between devices with their start and end apart: 18, of which 1 were waited for; matrix products, arithmetic and copies ran while one was open for 17% of the time, Pallas kernels for 0%

profile of v1, /device:TPU:2, one launch (start us, length us, event | category | flops | bytes accessed | tf_op | source)
XLA Modules:
  0.0 656.2 jit_solution(14613084394353494460)
XLA Ops:
  8.6 6.0 all-to-all-start
  15.4 24.0 %all_gather.10 = f32[8,2,2]{2,1,0:T(2,128)S(1)} all-gather(f32[1,2,2]{2,1,0:T(2,128)} %param.11), channel_id=1, replica_groups=mesh['span'=8,'tm'=32] {'span'}, dimensions={0}, use_global_device_ids=true | all-gather | bytes 144 | tf_op jit(solution)/shard_map/all_gather | solution.py:106
  39.4 18.4 %all_gather.11 = f32[8,2,110]{2,1,0:T(2,128)S(1)} all-gather(f32[1,2,110]{2,1,0:T(2,128)} %param.10), channel_id=1, replica_groups=mesh['span'=8,'tm'=32] {'span'}, dimensions={0}, use_global_device_ids=true | all-gather | bytes 7920 | tf_op jit(solution)/shard_map/all_gather | solution.py:105
  57.8 25.4 %all-gather.2.cloned.1.call-done = f32[8,2,2,2,110,110]{5,3,4,2,1,0:T(2,128)} async-done(((f32[1,2,2,2,110,110]{5,3,4,2,1,0:T(2,128)}), f32[8,2,2,2,110,110]{5,3,4,2,1,0:T(2,128)}) %all-gather.2.cloned.1.call-update) | async-done | bytes 3097616 | tf_op jit(solution)/shard_map/all_gather | solution.py:101
  83.3 538.8 %while.13 = (s32[]{:T(128)}, f32[1,2,110,256]{3,2,1,0:T(8,128)}, f32[8,1,2,110,256]{4,2,3,1,0:T(2,128)}, f32[8,2,2,2,129]{4,2,1,3,0:T(2,128)}, s32[]{:T(128)}, /...) while((s32[]{:T(128)}, f32[1,2,110,256]{3,2,1,0:T(8,128)}, ...), condition=%wide.region_5.6_spmd, body=%wide.region_0.5_spmd.sunk | while | flops 3470978304 | bytes 83235248 | solution.py:117
  83.3 4.8 collective-permute-start
  109.9 2.2 copy.115
  133.7 2.4 multiply_reduce_fusion.9
  149.8 5.7 collective-permute-start
  177.4 2.2 copy.115
  180.7 2.1 convolution_bitcast_fusion.12
  201.2 2.4 multiply_reduce_fusion.9
  217.3 5.8 collective-permute-start
  244.9 2.2 copy.115
  248.2 2.1 convolution_bitcast_fusion.12
  268.6 2.4 multiply_reduce_fusion.9
  284.8 5.7 collective-permute-start
  312.3 2.2 copy.115
  336.1 2.4 multiply_reduce_fusion.9
  352.2 5.8 collective-permute-start
  379.8 2.2 copy.115
  403.6 2.4 multiply_reduce_fusion.9
  419.7 5.7 collective-permute-start
  447.3 2.2 copy.115
  471.0 2.4 multiply_reduce_fusion.9
  487.1 5.8 collective-permute-start
  514.7 2.2 copy.115
  538.5 2.4 multiply_reduce_fusion.9
  554.6 5.7 collective-permute-start
  582.2 2.2 copy.115
  606.0 2.4 multiply_reduce_fusion.9
  622.1 26.1 %all_to_all.17 = f32[8,1,2,110,256]{4,2,3,1,0:T(2,128)S(1)} all-to-all(f32[8,1,2,110,256]{4,2,3,1,0:T(2,128)} %get-tuple-element.90), channel_id=1, replica_groups=mesh['span'=8,'tm'=32] {'span'}, dimensions={0} | all-to-all | bytes 3604480 | tf_op jit(solution)/shard_map/all_to_all | solution.py:120
  (889 shorter events, 452.5 us)
Async XLA Ops:
  6.5 8.1 %copy-start = (f32[8,2,110,256]{3,1,2,0:T(2,128)S(1)}, f32[8,2,110,256]{3,1,2,0:T(2,128)}, u32[]{:S(2)}) copy-start(f32[8,2,110,256]{3,1,2,0:T(2,128)} %param.7) | copy-start | bytes 5406724
  6.5 76.7 %all-gather.2.cloned.1.call-start = ((), (), s32[]{:S(2)}) async-start(), calls=%async_computation.2 | async-start | bytes 4055040 | tf_op jit(solution)/shard_map/all_gather | solution.py:101
  8.6 49.2 %all-to-all-start = ((f32[8,1,2,2,2,129]{5,3,2,4,1,0:T(2,128)}), f32[8,1,2,2,2,129]{5,3,2,4,1,0:T(2,128)}, u32[]{:S(2)}, u32[]{:S(2)}) async-start(f32[8,1,2,2,2,129]{5,3,2,4,1,0:T(2,128)} %stack.77), calls=%async_computation | async-start | bytes 131072 | tf_op jit(solution)/shard_map/all_to_all | solution.py:103
  83.3 20.6 %collective-permute-start = (f32[1,2,110,256]{3,2,1,0:T(8,128)}, f32[1,2,110,256]{3,2,1,0:T(8,128)}, u32[]{:S(2)}, u32[]{:S(2)}) collective-permute-start(f32[1,2,110,256]{3,2,1,0:T(8,128)} %get-tuple-element.367), channel_id=1, source_target_pairs={{1,0},{2,1},{3,2},{4,3},{5,4},{6,5},{7,6},{8,7},{9,8},{10,9},{11,1... | collective-permute-start | bytes 675848 | tf_op jit(solution)/shard_map/while/body/eval_jaxpr/ppermute | solution.py:68
  88.1 15.8 %collective-permute-start.1 = (f32[1,2,110,256]{3,2,1,0:T(8,128)}, f32[1,2,110,256]{3,2,1,0:T(8,128)}, u32[]{:S(2)}, u32[]{:S(2)}) collective-permute-start(f32[1,2,110,256]{3,2,1,0:T(8,128)} %get-tuple-element.367), channel_id=1, source_target_pairs={{0,1},{1,2},{2,3},{3,4},{4,5},{5,6},{6,7},{7,8},{8,9},{9,10},{10,1... | collective-permute-start | bytes 675848 | tf_op jit(solution)/shard_map/while/body/eval_jaxpr/ppermute | solution.py:67
  97.6 4.4 copy-start.1
  149.8 21.5 %collective-permute-start = (f32[1,2,110,256]{3,2,1,0:T(8,128)}, f32[1,2,110,256]{3,2,1,0:T(8,128)}, u32[]{:S(2)}, u32[]{:S(2)}) collective-permute-start(f32[1,2,110,256]{3,2,1,0:T(8,128)} %get-tuple-element.367), channel_id=1, source_target_pairs={{1,0},{2,1},{3,2},{4,3},{5,4},{6,5},{7,6},{8,7},{9,8},{10,9},{11,1... | collective-permute-start | bytes 675848 | tf_op jit(solution)/shard_map/while/body/eval_jaxpr/ppermute | solution.py:68
  155.6 15.8 %collective-permute-start.1 = (f32[1,2,110,256]{3,2,1,0:T(8,128)}, f32[1,2,110,256]{3,2,1,0:T(8,128)}, u32[]{:S(2)}, u32[]{:S(2)}) collective-permute-start(f32[1,2,110,256]{3,2,1,0:T(8,128)} %get-tuple-element.367), channel_id=1, source_target_pairs={{0,1},{1,2},{2,3},{3,4},{4,5},{5,6},{6,7},{7,8},{8,9},{9,10},{10,1... | collective-permute-start | bytes 675848 | tf_op jit(solution)/shard_map/while/body/eval_jaxpr/ppermute | solution.py:67
  165.1 4.4 copy-start.1
  168.7 2.3 copy-start.2
  217.3 21.5 %collective-permute-start = (f32[1,2,110,256]{3,2,1,0:T(8,128)}, f32[1,2,110,256]{3,2,1,0:T(8,128)}, u32[]{:S(2)}, u32[]{:S(2)}) collective-permute-start(f32[1,2,110,256]{3,2,1,0:T(8,128)} %get-tuple-element.367), channel_id=1, source_target_pairs={{1,0},{2,1},{3,2},{4,3},{5,4},{6,5},{7,6},{8,7},{9,8},{10,9},{11,1... | collective-permute-start | bytes 675848 | tf_op jit(solution)/shard_map/while/body/eval_jaxpr/ppermute | solution.py:68
  223.0 15.8 %collective-permute-start.1 = (f32[1,2,110,256]{3,2,1,0:T(8,128)}, f32[1,2,110,256]{3,2,1,0:T(8,128)}, u32[]{:S(2)}, u32[]{:S(2)}) collective-permute-start(f32[1,2,110,256]{3,2,1,0:T(8,128)} %get-tuple-element.367), channel_id=1, source_target_pairs={{0,1},{1,2},{2,3},{3,4},{4,5},{5,6},{6,7},{7,8},{8,9},{9,10},{10,1... | collective-permute-start | bytes 675848 | tf_op jit(solution)/shard_map/while/body/eval_jaxpr/ppermute | solution.py:67
  232.6 4.4 copy-start.1
  236.2 2.3 copy-start.2
  284.8 21.5 %collective-permute-start = (f32[1,2,110,256]{3,2,1,0:T(8,128)}, f32[1,2,110,256]{3,2,1,0:T(8,128)}, u32[]{:S(2)}, u32[]{:S(2)}) collective-permute-start(f32[1,2,110,256]{3,2,1,0:T(8,128)} %get-tuple-element.367), channel_id=1, source_target_pairs={{1,0},{2,1},{3,2},{4,3},{5,4},{6,5},{7,6},{8,7},{9,8},{10,9},{11,1... | collective-permute-start | bytes 675848 | tf_op jit(solution)/shard_map/while/body/eval_jaxpr/ppermute | solution.py:68
  290.5 15.8 %collective-permute-start.1 = (f32[1,2,110,256]{3,2,1,0:T(8,128)}, f32[1,2,110,256]{3,2,1,0:T(8,128)}, u32[]{:S(2)}, u32[]{:S(2)}) collective-permute-start(f32[1,2,110,256]{3,2,1,0:T(8,128)} %get-tuple-element.367), channel_id=1, source_target_pairs={{0,1},{1,2},{2,3},{3,4},{4,5},{5,6},{6,7},{7,8},{8,9},{9,10},{10,1... | collective-permute-start | bytes 675848 | tf_op jit(solution)/shard_map/while/body/eval_jaxpr/ppermute | solution.py:67
  300.0 4.4 copy-start.1
  303.6 2.3 copy-start.2
  352.2 21.5 %collective-permute-start = (f32[1,2,110,256]{3,2,1,0:T(8,128)}, f32[1,2,110,256]{3,2,1,0:T(8,128)}, u32[]{:S(2)}, u32[]{:S(2)}) collective-permute-start(f32[1,2,110,256]{3,2,1,0:T(8,128)} %get-tuple-element.367), channel_id=1, source_target_pairs={{1,0},{2,1},{3,2},{4,3},{5,4},{6,5},{7,6},{8,7},{9,8},{10,9},{11,1... | collective-permute-start | bytes 675848 | tf_op jit(solution)/shard_map/while/body/eval_jaxpr/ppermute | solution.py:68
  358.0 15.8 %collective-permute-start.1 = (f32[1,2,110,256]{3,2,1,0:T(8,128)}, f32[1,2,110,256]{3,2,1,0:T(8,128)}, u32[]{:S(2)}, u32[]{:S(2)}) collective-permute-start(f32[1,2,110,256]{3,2,1,0:T(8,128)} %get-tuple-element.367), channel_id=1, source_target_pairs={{0,1},{1,2},{2,3},{3,4},{4,5},{5,6},{6,7},{7,8},{8,9},{9,10},{10,1... | collective-permute-start | bytes 675848 | tf_op jit(solution)/shard_map/while/body/eval_jaxpr/ppermute | solution.py:67
  367.5 4.4 copy-start.1
  419.7 21.5 %collective-permute-start = (f32[1,2,110,256]{3,2,1,0:T(8,128)}, f32[1,2,110,256]{3,2,1,0:T(8,128)}, u32[]{:S(2)}, u32[]{:S(2)}) collective-permute-start(f32[1,2,110,256]{3,2,1,0:T(8,128)} %get-tuple-element.367), channel_id=1, source_target_pairs={{1,0},{2,1},{3,2},{4,3},{5,4},{6,5},{7,6},{8,7},{9,8},{10,9},{11,1... | collective-permute-start | bytes 675848 | tf_op jit(solution)/shard_map/while/body/eval_jaxpr/ppermute | solution.py:68
  425.4 15.8 %collective-permute-start.1 = (f32[1,2,110,256]{3,2,1,0:T(8,128)}, f32[1,2,110,256]{3,2,1,0:T(8,128)}, u32[]{:S(2)}, u32[]{:S(2)}) collective-permute-start(f32[1,2,110,256]{3,2,1,0:T(8,128)} %get-tuple-element.367), channel_id=1, source_target_pairs={{0,1},{1,2},{2,3},{3,4},{4,5},{5,6},{6,7},{7,8},{8,9},{9,10},{10,1... | collective-permute-start | bytes 675848 | tf_op jit(solution)/shard_map/while/body/eval_jaxpr/ppermute | solution.py:67
  434.9 4.4 copy-start.1
  487.1 21.5 %collective-permute-start = (f32[1,2,110,256]{3,2,1,0:T(8,128)}, f32[1,2,110,256]{3,2,1,0:T(8,128)}, u32[]{:S(2)}, u32[]{:S(2)}) collective-permute-start(f32[1,2,110,256]{3,2,1,0:T(8,128)} %get-tuple-element.367), channel_id=1, source_target_pairs={{1,0},{2,1},{3,2},{4,3},{5,4},{6,5},{7,6},{8,7},{9,8},{10,9},{11,1... | collective-permute-start | bytes 675848 | tf_op jit(solution)/shard_map/while/body/eval_jaxpr/ppermute | solution.py:68
  492.9 15.8 %collective-permute-start.1 = (f32[1,2,110,256]{3,2,1,0:T(8,128)}, f32[1,2,110,256]{3,2,1,0:T(8,128)}, u32[]{:S(2)}, u32[]{:S(2)}) collective-permute-start(f32[1,2,110,256]{3,2,1,0:T(8,128)} %get-tuple-element.367), channel_id=1, source_target_pairs={{0,1},{1,2},{2,3},{3,4},{4,5},{5,6},{6,7},{7,8},{8,9},{9,10},{10,1... | collective-permute-start | bytes 675848 | tf_op jit(solution)/shard_map/while/body/eval_jaxpr/ppermute | solution.py:67
  502.4 4.4 copy-start.1
  506.0 2.3 copy-start.2
  554.6 21.5 %collective-permute-start = (f32[1,2,110,256]{3,2,1,0:T(8,128)}, f32[1,2,110,256]{3,2,1,0:T(8,128)}, u32[]{:S(2)}, u32[]{:S(2)}) collective-permute-start(f32[1,2,110,256]{3,2,1,0:T(8,128)} %get-tuple-element.367), channel_id=1, source_target_pairs={{1,0},{2,1},{3,2},{4,3},{5,4},{6,5},{7,6},{8,7},{9,8},{10,9},{11,1... | collective-permute-start | bytes 675848 | tf_op jit(solution)/shard_map/while/body/eval_jaxpr/ppermute | solution.py:68
  560.4 15.8 %collective-permute-start.1 = (f32[1,2,110,256]{3,2,1,0:T(8,128)}, f32[1,2,110,256]{3,2,1,0:T(8,128)}, u32[]{:S(2)}, u32[]{:S(2)}) collective-permute-start(f32[1,2,110,256]{3,2,1,0:T(8,128)} %get-tuple-element.367), channel_id=1, source_target_pairs={{0,1},{1,2},{2,3},{3,4},{4,5},{5,6},{6,7},{7,8},{8,9},{9,10},{10,1... | collective-permute-start | bytes 675848 | tf_op jit(solution)/shard_map/while/body/eval_jaxpr/ppermute | solution.py:67
  569.9 4.4 copy-start.1
  573.5 2.3 copy-start.2
  (19 other events, 43.1 us)
Sparse Core Ops, SparseCore 0:
  9.9 73.2 all-gather.1
